TPU v7x, 256 devices: a whole 4x4x8 slice. The times are simulated.
256 devices in a mesh: grp: 8 (over x, core), cell: 32 (over y, z).
Axes of the slice: x: 4, y: 4, z: 8, core: 2. Of those that a mesh axis runs over, the one named last changes fastest.
Arguments:
- rhs: float32 [128, 2, 128, 16, 128], P('grp', None, 'cell'), may hold values from -8 to 8
- log_perm: float32 [128, 128, 16, 128], P('grp', 'cell'), may hold values from -1.5 to 1.5
- porosity: float32 [128, 128, 16, 128], P('grp', 'cell'), may hold values from 0.1 to 0.3
- saturation: float32 [128, 128, 16, 128], P('grp', 'cell'), may hold values from 0.2 to 0.8
- pressure: float32 [128, 128, 16, 128], P('grp', 'cell'), may hold values from -6 to 6
- obs_values: float32 [256], replicated, may hold values from -6 to 6
- obs_error: float32 [256], replicated, may hold values from 0.1 to 1
- noise: float32 [128, 256], replicated, may hold values from -6 to 6
- well_cell: int32 [128], replicated, may hold values from 0 to 262143
- obs_well: int32 [256], replicated, may hold values from 0 to 127
Outputs:
- increment: float32 [128, 2, 128, 16, 128], P('grp', None, 'cell')
- log_perm_post: float32 [128, 128, 16, 128], P('grp', 'cell')
- porosity_post: float32 [128, 128, 16, 128], P('grp', 'cell')
All inputs are finite; a program needn't handle non-finite values.
Results may differ from a plain program's by a relative error of at most 0.0003.
Values sent between devices are 32-bit elements; how exact they have to be, the bound alone decides.
No kernel may reach another device: no remote copies, remote signals or barrier semaphores. Data moves between devices by JAX's collectives and lax.ppermute only.
A program may use at most 128 MiB of HBM per device.

v0:
```python
import math
import jax
import jax.numpy as jnp
from jax import lax
from jax.sharding import PartitionSpec as P

KRYLOV = 4
epsilon = 1e-06
time_step = 0.1
compress = 0.5
inflation = 4.0


def with_halo(block, sides, width):
    for axis, dim in sides:
        count = lax.axis_size(axis)
        forward = [(i, i + 1) for i in range(count - 1)]
        backward = [(target, source) for source, target in forward]
        low = lax.ppermute(
            lax.slice_in_dim(block, block.shape[dim] - width, None, axis=dim), axis, forward
        )
        high = lax.ppermute(lax.slice_in_dim(block, 0, width, axis=dim), axis, backward)
        block = jnp.concatenate([low, block, high], axis=dim)
    return block


def mobility(sat_field):
    return sat_field * sat_field + 0.5 * (1.0 - sat_field) * (1.0 - sat_field)


def face_pair(perm_low, perm_high, sat_low, sat_high):
    trans = (
        2.0
        * perm_low
        * perm_high
        / (perm_low + perm_high)
        * (0.5 * (mobility(sat_low) + mobility(sat_high)))
    )
    return (trans, trans * (0.5 * (sat_low + sat_high)))


def plane_faces(perm, sat_field):
    plane_rows = perm.shape[-2]
    plane_cols = perm.shape[-1]
    keep_rows = (
        lax.broadcasted_iota(jnp.int32, (plane_rows, plane_cols), 0) < plane_rows - 1
    ).astype(jnp.float32)
    keep_cols = (
        lax.broadcasted_iota(jnp.int32, (plane_rows, plane_cols), 1) < plane_cols - 1
    ).astype(jnp.float32)
    trans_y, frac_y = face_pair(
        perm, jnp.roll(perm, -1, -2), sat_field, jnp.roll(sat_field, -1, -2)
    )
    trans_z, frac_z = face_pair(
        perm, jnp.roll(perm, -1, -1), sat_field, jnp.roll(sat_field, -1, -1)
    )
    return (trans_y * keep_rows, frac_y * keep_rows, trans_z * keep_cols, frac_z * keep_cols)


def operator(padded, second, coeffs):
    accum, trans_x, frac_x, trans_y, frac_y, trans_z, frac_z = coeffs
    first = padded[..., 1:-1, :, :]
    diff_x = padded[..., 1:, :, :] - padded[..., :-1, :, :]
    diff_y = jnp.roll(first, -1, -2) - first
    diff_z = jnp.roll(first, -1, -1) - first

    def net(coef_x, coef_y, coef_z):
        flow_x = coef_x * diff_x
        flow_y = coef_y * diff_y
        flow_z = coef_z * diff_z
        return (
            flow_x[..., :-1, :, :]
            - flow_x[..., 1:, :, :]
            + (jnp.roll(flow_y, 1, -2) - flow_y)
            + (jnp.roll(flow_z, 1, -1) - flow_z)
        )

    out_pressure = accum * (compress * first + 0.5 * second) + net(trans_x, trans_y, trans_z)
    out_water = accum * second + net(frac_x, frac_y, frac_z)
    return (out_pressure, out_water)


def least_squares(columns, beta):
    rows = [list(column) for column in columns]
    cosines = []
    sines = []
    target = [beta] + [jnp.zeros_like(beta) for column in columns]
    for jdx in range(len(rows)):
        column = rows[jdx]
        for idx in range(jdx):
            upper = cosines[idx] * column[idx] + sines[idx] * column[idx + 1]
            column[idx + 1] = -sines[idx] * column[idx] + cosines[idx] * column[idx + 1]
            column[idx] = upper
        radius = jnp.sqrt(column[jdx] * column[jdx] + column[jdx + 1] * column[jdx + 1])
        cosines.append(column[jdx] / radius)
        sines.append(column[jdx + 1] / radius)
        column[jdx] = radius
        target[jdx + 1] = -sines[jdx] * target[jdx]
        target[jdx] = cosines[jdx] * target[jdx]
    count = len(rows)
    solved = [None] * count
    for jdx in reversed(range(count)):
        partial_sum = target[jdx]
        for idx in range(jdx + 1, count):
            partial_sum = partial_sum - rows[idx][jdx] * solved[idx]
        solved[jdx] = partial_sum / rows[jdx][jdx]
    return solved


def ensemble_weights(predicted, obs_values, obs_error, noise):
    members = predicted.shape[0]
    sigma = math.sqrt(inflation) * obs_error
    center = jnp.mean(predicted, axis=0)
    spread = (predicted - center) / (math.sqrt(members - 1.0) * sigma)
    innov = (obs_values + sigma * noise - predicted) / sigma
    gram = jnp.eye(members, dtype=jnp.float32) + jnp.dot(
        spread, spread.T, precision=lax.Precision.HIGHEST, preferred_element_type=jnp.float32
    )
    cross = jnp.dot(
        spread, innov.T, precision=lax.Precision.HIGHEST, preferred_element_type=jnp.float32
    )
    factor = jnp.linalg.cholesky(gram)
    return jax.scipy.linalg.cho_solve((factor, True), cross)


def expand(values):
    return values[:, None, None, None, None]


def inner(left, right):
    return jnp.sum(left * right, axis=(1, 2, 3, 4))


def local(
    rhs, log_perm, porosity, saturation, pressure, obs_values, obs_error, noise, well_cell, obs_well
):
    local_members, slab_x, plane_rows, plane_cols = log_perm.shape
    members = noise.shape[0]
    plane = plane_rows * plane_cols
    cells_dev = slab_x * plane
    slab_index = lax.axis_index("cell")
    slab_count = lax.axis_size("cell")
    stacked = jnp.stack([log_perm, saturation], axis=1)
    rimmed = with_halo(stacked, (("cell", 2),), 1)
    perm_pad = jnp.exp(rimmed[:, 0])
    sat_pad = rimmed[:, 1]
    trans_x, frac_x = face_pair(perm_pad[:, :-1], perm_pad[:, 1:], sat_pad[:, :-1], sat_pad[:, 1:])
    face_pos = lax.broadcasted_iota(jnp.int32, (slab_x + 1, 1, 1), 0)
    keep_face = jnp.where(
        face_pos == 0,
        slab_index > 0,
        jnp.where(face_pos == slab_x, slab_index < slab_count - 1, True),
    ).astype(jnp.float32)
    trans_x = trans_x * keep_face
    frac_x = frac_x * keep_face
    trans_y, frac_y, trans_z, frac_z = plane_faces(perm_pad[:, 1:-1], saturation)
    coeffs = (porosity / time_step, trans_x, frac_x, trans_y, frac_y, trans_z, frac_z)
    columns = []
    beta = jnp.sqrt(lax.psum(inner(rhs, rhs), "cell") + epsilon)
    basis = [rhs / expand(beta)]
    for jdx in range(KRYLOV):
        vector = basis[jdx]
        padded = with_halo(vector[:, 0], (("cell", 1),), 1)
        out_pressure, out_water = operator(padded, vector[:, 1], coeffs)
        image = jnp.stack([out_pressure, out_water], 1)
        local_dots = jnp.stack([inner(basis[idx], image) for idx in range(jdx + 1)], 0)
        projected = lax.psum(local_dots, "cell")
        for idx in range(jdx + 1):
            image = image - expand(projected[idx]) * basis[idx]
        height = jnp.sqrt(lax.psum(inner(image, image), "cell") + epsilon)
        columns.append([projected[idx] for idx in range(jdx + 1)] + [height])
        basis.append(image / expand(height))
    solved = least_squares(columns, beta)
    increment = expand(solved[0]) * basis[0]
    for jdx in range(1, KRYLOV):
        increment = increment + expand(solved[jdx]) * basis[jdx]
    flat = jnp.stack([pressure + increment[:, 0], saturation + increment[:, 1]], 1).reshape(
        local_members, 2 * cells_dev
    )
    cells = jnp.take(well_cell, obs_well)
    wells = well_cell.shape[0]
    component = (jnp.arange(obs_well.shape[0], dtype=jnp.int32) >= wells).astype(jnp.int32)
    slab_row = cells // plane - slab_index * slab_x
    inside = (slab_row >= 0) & (slab_row < slab_x)
    local_cell = jnp.where(inside, slab_row * plane + cells % plane, 0)
    picked = jnp.take(flat, component * cells_dev + local_cell, axis=1) * inside.astype(jnp.float32)
    slab_pred = lax.psum(picked, "cell")
    predicted = lax.all_gather(slab_pred, "grp", axis=0, tiled=True)
    weights = ensemble_weights(predicted, obs_values, obs_error, noise)
    params = jnp.stack([log_perm, porosity], 1).reshape(local_members, 2 * cells_dev)
    offset = lax.axis_index("grp") * local_members
    scale_factor = 1.0 / math.sqrt(members - 1.0)
    scaled = params * scale_factor
    own_columns = lax.dynamic_slice_in_dim(weights, offset, local_members, 1)
    update = jnp.dot(
        own_columns.T,
        lax.all_gather(scaled, "grp", axis=0, tiled=True),
        precision=lax.Precision.HIGHEST,
        preferred_element_type=jnp.float32,
    )
    posterior = params + update
    posterior = posterior.reshape(local_members, 2, slab_x, plane_rows, plane_cols)
    return (increment, posterior[:, 0], posterior[:, 1])


def solution(mesh):
    in_specs = (
        P("grp", None, "cell", None, None),
        P("grp", "cell", None, None),
        P("grp", "cell", None, None),
        P("grp", "cell", None, None),
        P("grp", "cell", None, None),
        P(),
        P(),
        P(),
        P(),
        P(),
    )
    out_specs = (
        P("grp", None, "cell", None, None),
        P("grp", "cell", None, None),
        P("grp", "cell", None, None),
    )
    return jax.shard_map(local, mesh=mesh, in_specs=in_specs, out_specs=out_specs, check_vma=False)
```

profile of v0, /device:TPU:1, one launch (start us, length us, event | category | flops | bytes accessed | tf_op | source)
XLA Modules:
  0.0 937.8 jit_solution(11814738720340162796)
XLA Ops:
  7.2 2.0 fusion.61
  9.3 4.5 collective-permute-start
  14.0 1.3 collective-permute-start.1
  15.3 64.8 %psum.70 = f32[16]{0:T(128)S(1)} all-reduce(f32[16]{0:T(128)S(1)} %multiply_reduce_fusion.14), channel_id=1, replica_groups=mesh['grp'=8,'cell'=32] {'cell'}, use_global_device_ids=true, to_apply=%region_1.2 | all-reduce | flops 16 | bytes 128 | tf_op jit(solution)/shard_map/psum | solution.py:159
  80.3 0.7 fusion.108
  81.0 1.3 collective-permute-start.2
  82.3 4.7 collective-permute-start.3
  87.1 1.0 copy-done.22
  88.1 1.7 bitcast_multiply_fusion
  89.9 1.9 gather_fusion
  91.9 0.8 slice.516
  92.7 1.0 slice.522
  93.7 0.9 slice.402
  94.6 1.0 slice.410
  95.7 1.1 pad_maximum_fusion
  97.3 0.7 copy-done.31
  98.5 1.1 multiply_multiply_fusion.11
  99.6 1.6 fusion.100
  101.7 2.7 fusion.60
  104.4 0.6 fusion.52
  106.6 55.7 %psum.71 = f32[16]{0:T(128)S(1)} all-reduce(f32[16]{0:T(128)S(1)} %multiply_reduce_fusion.13), channel_id=1, replica_groups=mesh['grp'=8,'cell'=32] {'cell'}, use_global_device_ids=true, to_apply=%region_3.4 | all-reduce | flops 16 | bytes 128 | tf_op jit(solution)/shard_map/psum | solution.py:167
  162.3 1.6 multiply_reduce_fusion.12
  163.9 57.9 %psum.72 = f32[16]{0:T(128)S(1)} all-reduce(f32[16]{0:T(128)S(1)} %get-tuple-element.23), channel_id=1, replica_groups=mesh['grp'=8,'cell'=32] {'cell'}, use_global_device_ids=true, to_apply=%region_5.6 | all-reduce | flops 16 | bytes 128 | tf_op jit(solution)/shard_map/psum | solution.py:170
  222.3 1.4 collective-permute-start.4
  223.7 4.0 collective-permute-start.5
  227.8 0.6 multiply_multiply_fusion.10
  228.8 0.8 collective-permute-done.5
  229.8 0.5 fusion.40
  230.4 0.6 fusion.44
  232.0 57.7 %psum.73 = f32[2,16]{1,0:T(2,128)S(1)} all-reduce(f32[2,16]{1,0:T(2,128)S(1)} %pad_maximum_fusion.14), channel_id=1, replica_groups=mesh['grp'=8,'cell'=32] {'cell'}, use_global_device_ids=true, to_apply=%region_8.9 | all-reduce | flops 32 | bytes 256 | tf_op jit(solution)/shard_map/psum | solution.py:167
  289.7 1.7 multiply_reduce_fusion.9
  291.4 55.7 %psum.74 = f32[16]{0:T(128)S(1)} all-reduce(f32[16]{0:T(128)S(1)} %get-tuple-element.21), channel_id=1, replica_groups=mesh['grp'=8,'cell'=32] {'cell'}, use_global_device_ids=true, to_apply=%region_10.11 | all-reduce | flops 16 | bytes 128 | tf_op jit(solution)/shard_map/psum | solution.py:170
  347.6 1.4 collective-permute-start.6
  349.0 4.2 collective-permute-start.7
  353.2 0.6 multiply_multiply_fusion.9
  354.4 0.6 collective-permute-done.7
  356.0 0.6 fusion.36
  356.8 0.6 multiply_reduce_fusion.8
  357.6 57.3 %psum.75 = f32[3,16]{1,0:T(4,128)S(1)} all-reduce(f32[3,16]{1,0:T(4,128)S(1)} %pad_maximum_fusion.12), channel_id=1, replica_groups=mesh['grp'=8,'cell'=32] {'cell'}, use_global_device_ids=true, to_apply=%region_14.15 | all-reduce | flops 48 | bytes 384 | tf_op jit(solution)/shard_map/psum | solution.py:167
  414.9 2.7 multiply_reduce_fusion.5
  417.6 56.2 %psum.76 = f32[16]{0:T(128)S(1)} all-reduce(f32[16]{0:T(128)S(1)} %get-tuple-element.19), channel_id=1, replica_groups=mesh['grp'=8,'cell'=32] {'cell'}, use_global_device_ids=true, to_apply=%region_16.17 | all-reduce | flops 16 | bytes 128 | tf_op jit(solution)/shard_map/psum | solution.py:170
  473.8 1.4 copy_divide_fusion
  475.6 1.4 collective-permute-start.8
  477.0 4.1 collective-permute-start.9
  481.2 0.6 multiply_multiply_fusion.8
  482.3 0.8 collective-permute-done.9
  483.5 0.5 fusion.28
  484.8 0.6 copy-done.8
  485.4 0.7 multiply_reduce_fusion.4
  486.2 57.4 %psum.77 = f32[4,16]{1,0:T(4,128)S(1)} all-reduce(f32[4,16]{1,0:T(4,128)S(1)} %pad_maximum_fusion.13), channel_id=1, replica_groups=mesh['grp'=8,'cell'=32] {'cell'}, use_global_device_ids=true, to_apply=%region_21.22 | all-reduce | flops 64 | bytes 512 | tf_op jit(solution)/shard_map/psum | solution.py:167
  543.6 2.2 multiply_reduce_fusion
  545.8 56.0 %psum.78 = f32[16]{0:T(128)S(1)} all-reduce(f32[16]{0:T(128)S(1)} %multiply_reduce_fusion), channel_id=1, replica_groups=mesh['grp'=8,'cell'=32] {'cell'}, use_global_device_ids=true, to_apply=%region_23.24 | all-reduce | flops 16 | bytes 128 | tf_op jit(solution)/shard_map/psum | solution.py:170
  602.0 1.8 multiply_add_fusion
  604.0 0.8 copy-done.43
  604.9 4.6 copy.101
  609.5 4.1 gather_fusion.1
  613.8 111.5 %psum.79 = f32[16,256]{0,1:T(8,128)S(1)} all-reduce(f32[16,256]{0,1:T(8,128)S(1)} %multiply_bitcast_fusion), channel_id=1, replica_groups=mesh['grp'=8,'cell'=32] {'cell'}, use_global_device_ids=true, to_apply=%region_24.25 | all-reduce | flops 4096 | bytes 32768 | tf_op jit(solution)/shard_map/psum | solution.py:187
  725.3 173.0 %all_gather.6 = f32[128,256]{1,0:T(8,128)S(1)} all-gather(f32[16,256]{1,0:T(8,128)S(1)} %copy.102), channel_id=1, replica_groups=mesh['grp'=8,'cell'=32] {'grp'}, dimensions={0}, use_global_device_ids=true | all-gather | bytes 147456 | tf_op jit(solution)/shard_map/all_gather | solution.py:188
  898.8 11.7 %cholesky.17 = f32[128,128]{1,0:T(8,128)S(1)} custom-call(f32[128,128]{1,0:T(8,128)S(1)} %fusion.78), custom_call_target="Cholesky" | custom-call | tf_op jit(solution)/shard_map/jit(cholesky)/cholesky | solution.py:122
  910.5 0.6 compare_reduce_fusion
  911.2 0.7 fusion.72
  911.8 9.8 %custom-call.10 = f32[1,128,128]{1,2,0:T(8,128)S(1)} custom-call(f32[1,128,128]{2,1,0:T(8,128)S(1)} %fusion.72), custom_call_target="InvertDiagBlocksLowerTriangular" | custom-call | tf_op jit(solution)/shard_map/jit(_cho_solve)/triangular_solve | solution.py:123
  922.6 7.1 fusion
  929.9 1.1 slice_bitcast_fusion.1
  (188 shorter events, 12.4 us)
Async XLA Ops:
  7.2 82.7 %copy-start = (s32[128]{0:T(128)S(1)}, s32[128]{0:T(128)}, u32[]{:S(2)}) copy-start(s32[128]{0:T(128)} %param.18) | copy-start | bytes 1540
  7.2 6.6 copy-start.2
  7.2 915.4 %all-gather.2.cloned.1.call-start = ((), (), s32[]{:S(2)}) async-start(), calls=%async_computation | async-start | bytes 9437184 | tf_op jit(solution)/shard_map/all_gather | solution.py:197
  9.3 77.7 %copy-start.5 = (f32[16,4,16,128]{3,2,1,0:T(8,128)S(1)}, f32[16,4,16,128]{3,2,1,0:T(8,128)}, u32[]{:S(2)}) copy-start(f32[16,4,16,128]{3,2,1,0:T(8,128)} %param.12) | copy-start | bytes 1572868
  9.3 77.7 %copy-start.37 = (f32[16,4,16,128]{3,2,1,0:T(8,128)S(1)}, f32[16,4,16,128]{3,2,1,0:T(8,128)}, u32[]{:S(2)}) copy-start(f32[16,4,16,128]{3,2,1,0:T(8,128)} %param.11) | copy-start | bytes 1572868
  9.3 86.4 %collective-permute-start = (f32[16,2,1,16,128]{4,3,2,0,1:T(8,128)}, f32[16,2,1,16,128]{4,3,2,0,1:T(8,128)S(1)}, u32[]{:S(2)}, u32[]{:S(2)}) collective-permute-start(f32[16,2,1,16,128]{4,3,2,0,1:T(8,128)} %get-tuple-element.67), channel_id=1, source_target_pairs={{0,1},{1,2},{2,3},{3,4},{4,5},{5,6},{6,7},{7,8},{8,9},{9,10},{10,1... | collective-permute-start | bytes 786440 | tf_op jit(solution)/shard_map/ppermute | solution.py:19
  14.0 81.7 %collective-permute-start.1 = (f32[16,2,1,16,128]{4,3,2,0,1:T(8,128)}, f32[16,2,1,16,128]{4,3,2,0,1:T(8,128)}, u32[]{:S(2)}, u32[]{:S(2)}) collective-permute-start(f32[16,2,1,16,128]{4,3,2,0,1:T(8,128)} %get-tuple-element.68), channel_id=1, source_target_pairs={{1,0},{2,1},{3,2},{4,3},{5,4},{6,5},{7,6},{8,7},{9,8},{10,9},{11,1... | collective-permute-start | bytes 786440 | tf_op jit(solution)/shard_map/ppermute | solution.py:22
  81.0 20.7 %collective-permute-start.2 = (f32[16,1,16,128]{3,2,1,0:T(8,128)}, f32[16,1,16,128]{3,2,1,0:T(8,128)}, u32[]{:S(2)}, u32[]{:S(2)}) collective-permute-start(f32[16,1,16,128]{3,2,1,0:T(8,128)} %get-tuple-element.81), channel_id=1, source_target_pairs={{1,0},{2,1},{3,2},{4,3},{5,4},{6,5},{7,6},{8,7},{9,8},{10,9},{11,1... | collective-permute-start | bytes 393224 | tf_op jit(solution)/shard_map/ppermute | solution.py:22
  82.3 19.4 %collective-permute-start.3 = (f32[16,1,16,128]{3,2,1,0:T(8,128)}, f32[16,1,16,128]{3,2,1,0:T(8,128)}, u32[]{:S(2)}, u32[]{:S(2)}) collective-permute-start(f32[16,1,16,128]{3,2,1,0:T(8,128)} %get-tuple-element.82), channel_id=1, source_target_pairs={{0,1},{1,2},{2,3},{3,4},{4,5},{5,6},{6,7},{7,8},{8,9},{9,10},{10,1... | collective-permute-start | bytes 393224 | tf_op jit(solution)/shard_map/ppermute | solution.py:19
  87.1 1.0 copy-start.22
  88.1 1.8 copy-start.45
  89.9 3.8 copy-start.3
  92.7 2.9 copy-start.46
  96.9 1.0 copy-start.31
  96.9 1.2 copy-start.32
  97.0 1.3 copy-start.33
  97.0 1.5 copy-start.34
  99.6 1.6 copy-start.12
  99.6 128.1 %copy-start.9 = (f32[16,4,16,128]{3,2,1,0:T(8,128)}, f32[16,4,16,128]{3,2,1,0:T(8,128)S(1)}, u32[]{:S(2)}) copy-start(f32[16,4,16,128]{3,2,1,0:T(8,128)S(1)} %get-tuple-element.26) | copy-start | bytes 1572868
  105.0 0.8 copy-start.35
  105.8 0.8 copy-start.36
  221.9 5.8 copy-start.13
  222.0 5.8 copy-start.24
  222.0 5.8 copy-start.27
  222.3 6.5 collective-permute-start.4
  223.7 5.9 collective-permute-start.5
  228.3 1.3 copy-start.16
  228.3 1.3 copy-start.19
  230.4 0.8 copy-start.41
  231.2 0.8 copy-start.42
  347.2 6.0 copy-start.10
  347.2 6.0 copy-start.14
  347.2 6.0 copy-start.25
  347.2 6.0 copy-start.28
  347.6 6.8 collective-permute-start.6
  349.0 6.0 collective-permute-start.7
  353.9 1.1 copy-start.17
  353.9 1.3 copy-start.20
  354.4 1.1 copy-start.6
  356.0 0.8 copy-start.39
  356.8 0.8 copy-start.40
  475.3 5.9 copy-start.11
  475.3 5.9 copy-start.15
  475.3 5.9 copy-start.26
  475.3 5.9 copy-start.29
  475.6 6.7 collective-permute-start.8
  477.0 6.1 collective-permute-start.9
  481.8 1.3 copy-start.18
  481.8 1.3 copy-start.21
  482.3 1.1 copy-start.7
  484.0 0.8 copy-start.38
  484.0 1.4 copy-start.8
  485.4 0.8 copy-start.30
  601.9 1.8 copy-start.4
  601.9 1.8 copy-start.44
  603.8 1.0 copy-start.43
  609.5 312.2 %copy-start.47 = (f32[128,256]{1,0:T(8,128)S(1)}, f32[128,256]{1,0:T(8,128)}, u32[]{:S(2)}) copy-start(f32[128,256]{1,0:T(8,128)} %param.17) | copy-start | bytes 393220
  609.5 312.2 %copy-start.48 = (f32[256]{0:T(256)S(1)}, f32[256]{0:T(256)}, u32[]{:S(2)}) copy-start(f32[256]{0:T(256)} %param.15) | copy-start | bytes 3076
  613.8 308.8 %copy-start.23 = (f32[16,2,4,16,128]{4,3,2,1,0:T(8,128)S(1)}, f32[16,2,4,16,128]{4,3,2,1,0:T(8,128)}, u32[]{:S(2)}) copy-start(f32[16,2,4,16,128]{4,3,2,1,0:T(8,128)} %copy-done.22) | copy-start | bytes 3145732
  929.7 1.3 copy-start.1
Sparse Core Ops, SparseCore 0:
  89.9 61.6 all-gather.1
where the time goes:
time: 939 us; the launch traced here: 938 us
  blocking collectives  803 us (86%)
  other arithmetic  54.4 us (6%)
  starting transfers between devices  28.3 us (3%)
  local copies, waits for them, and re-layouts  26.2 us (3%)
  between operations  15.2 us (2%)
    psum x4, blocking collectives, local(): projected = lax.psum(local_dots, 'cell')  228 us
    psum x4, blocking collectives, local(): height = jnp.sqrt(lax.psum(inner(image, image), 'cell') + epsilon)  226 us
    all_gather x1, blocking collectives, local(): predicted = lax.all_gather(slab_pred, 'grp', axis=0, tiled=True)  173 us
    psum x1, blocking collectives, local(): slab_pred = lax.psum(picked, 'cell')  111 us
    psum x1, blocking collectives, local(): beta = jnp.sqrt(lax.psum(inner(rhs, rhs), 'cell') + epsilon)  64.8 us
    ppermute x5, starting transfers between devices, with_halo(): lax.ppermute(lax.slice_in_dim(block, block.shape[dim] - width, None, axis...  21.5 us
  transfers between devices with their start and end apart: 11, of which 3 were waited for; matrix products, arithmetic and copies ran while one was open for 8% of the time, Pallas kernels for 0%

commit v1 on v0

--- a/solution.py
+++ b/solution.py
@@ -9,6 +9,7 @@
 time_step = 0.1
 compress = 0.5
 inflation = 4.0
+_take_files = lambda xin: lax.all_gather(xin, "cell").sum(axis=0)
 
 
 def with_halo(block, sides, width):
@@ -184,7 +185,7 @@
     inside = (slab_row >= 0) & (slab_row < slab_x)
     local_cell = jnp.where(inside, slab_row * plane + cells % plane, 0)
     picked = jnp.take(flat, component * cells_dev + local_cell, axis=1) * inside.astype(jnp.float32)
-    slab_pred = lax.psum(picked, "cell")
+    slab_pred = _take_files(picked)
     predicted = lax.all_gather(slab_pred, "grp", axis=0, tiled=True)
     weights = ensemble_weights(predicted, obs_values, obs_error, noise)
     params = jnp.stack([log_perm, porosity], 1).reshape(local_members, 2 * cells_dev)

time: 939 us -> 847 us (0.902)
  blocking collectives: 803 us -> 712 us
    psum x1 -> x0, blocking collectives: 111 us -> none  [local(): slab_pred = lax.psum(picked, 'cell')]
    all_gather x0 -> x1, blocking collectives: none -> 36.3 us  [_take_files = lambda xin: lax.all_gather(xin, 'cell').sum(axis=0)]
    all_gather x1, blocking collectives: 173 us -> 157 us  [local(): predicted = lax.all_gather(slab_pred, 'grp', axis=0, tiled=True)]
  transfers between devices with their start and end apart: 11 -> 11, of which waited for: 3 -> 3; matrix products, arithmetic and copies ran while one was open for 8% -> 9% of each run, Pallas kernels for 0% -> 0%
where the time goes in v1:
time: 847 us; the launch traced here: 846 us
  blocking collectives  712 us (84%)
  other arithmetic  54.3 us (6%)
  starting transfers between devices  28.3 us (3%)
  local copies, waits for them, and re-layouts  26.2 us (3%)
  between operations  15.2 us (2%)
    psum x4, blocking collectives, local(): projected = lax.psum(local_dots, 'cell')  228 us
    psum x4, blocking collectives, local(): height = jnp.sqrt(lax.psum(inner(image, image), 'cell') + epsilon)  226 us
    all_gather x1, blocking collectives, local(): predicted = lax.all_gather(slab_pred, 'grp', axis=0, tiled=True)  157 us
    psum x1, blocking collectives, local(): beta = jnp.sqrt(lax.psum(inner(rhs, rhs), 'cell') + epsilon)  64.8 us
    all_gather x1, blocking collectives, _take_files = lambda xin: lax.all_gather(xin, 'cell').sum(axis=0)  36.3 us
    ppermute x5, starting transfers between devices, with_halo(): lax.ppermute(lax.slice_in_dim(block, block.shape[dim] - width, None, axis...  21.5 us
  transfers between devices with their start and end apart: 11, of which 3 were waited for; matrix products, arithmetic and copies ran while one was open for 9% of the time, Pallas kernels for 0%

profile of v1, /device:TPU:1, one launch (start us, length us, event | category | flops | bytes accessed | tf_op | source)
XLA Modules:
  0.0 846.2 jit_solution(4321830589068722195)
XLA Ops:
  7.2 2.0 fusion.61
  9.3 4.5 collective-permute-start
  14.0 1.3 collective-permute-start.1
  15.3 64.8 %psum.63 = f32[16]{0:T(128)S(1)} all-reduce(f32[16]{0:T(128)S(1)} %multiply_reduce_fusion.14), channel_id=1, replica_groups=mesh['grp'=8,'cell'=32] {'cell'}, use_global_device_ids=true, to_apply=%region_1.2 | all-reduce | flops 16 | bytes 128 | tf_op jit(solution)/shard_map/psum | solution.py:160
  80.3 0.7 fusion.109
  81.0 1.3 collective-permute-start.2
  82.3 4.7 collective-permute-start.3
  87.1 1.0 copy-done.22
  88.1 1.7 bitcast_multiply_fusion
  89.9 1.9 gather_fusion
  91.9 0.8 slice.516
  92.7 1.0 slice.522
  93.7 0.9 slice.402
  94.6 1.0 slice.410
  95.7 1.1 pad_maximum_fusion
  97.3 0.7 copy-done.31
  98.5 1.1 multiply_multiply_fusion.11
  99.6 1.6 fusion.101
  101.7 2.7 fusion.60
  104.4 0.6 fusion.52
  106.5 55.7 %psum.64 = f32[16]{0:T(128)S(1)} all-reduce(f32[16]{0:T(128)S(1)} %multiply_reduce_fusion.13), channel_id=1, replica_groups=mesh['grp'=8,'cell'=32] {'cell'}, use_global_device_ids=true, to_apply=%region_3.4 | all-reduce | flops 16 | bytes 128 | tf_op jit(solution)/shard_map/psum | solution.py:168
  162.3 1.6 multiply_reduce_fusion.12
  163.9 57.9 %psum.65 = f32[16]{0:T(128)S(1)} all-reduce(f32[16]{0:T(128)S(1)} %get-tuple-element.23), channel_id=1, replica_groups=mesh['grp'=8,'cell'=32] {'cell'}, use_global_device_ids=true, to_apply=%region_5.6 | all-reduce | flops 16 | bytes 128 | tf_op jit(solution)/shard_map/psum | solution.py:171
  222.3 1.4 collective-permute-start.4
  223.7 4.0 collective-permute-start.5
  227.7 0.6 multiply_multiply_fusion.10
  228.8 0.8 collective-permute-done.5
  229.8 0.5 fusion.40
  230.4 0.6 fusion.44
  232.0 57.7 %psum.66 = f32[2,16]{1,0:T(2,128)S(1)} all-reduce(f32[2,16]{1,0:T(2,128)S(1)} %pad_maximum_fusion.14), channel_id=1, replica_groups=mesh['grp'=8,'cell'=32] {'cell'}, use_global_device_ids=true, to_apply=%region_8.9 | all-reduce | flops 32 | bytes 256 | tf_op jit(solution)/shard_map/psum | solution.py:168
  289.7 1.7 multiply_reduce_fusion.9
  291.4 55.7 %psum.67 = f32[16]{0:T(128)S(1)} all-reduce(f32[16]{0:T(128)S(1)} %get-tuple-element.21), channel_id=1, replica_groups=mesh['grp'=8,'cell'=32] {'cell'}, use_global_device_ids=true, to_apply=%region_10.11 | all-reduce | flops 16 | bytes 128 | tf_op jit(solution)/shard_map/psum | solution.py:171
  347.6 1.4 collective-permute-start.6
  349.0 4.2 collective-permute-start.7
  353.2 0.6 multiply_multiply_fusion.9
  354.4 0.6 collective-permute-done.7
  356.0 0.6 fusion.36
  356.8 0.6 multiply_reduce_fusion.8
  357.6 57.3 %psum.68 = f32[3,16]{1,0:T(4,128)S(1)} all-reduce(f32[3,16]{1,0:T(4,128)S(1)} %pad_maximum_fusion.12), channel_id=1, replica_groups=mesh['grp'=8,'cell'=32] {'cell'}, use_global_device_ids=true, to_apply=%region_14.15 | all-reduce | flops 48 | bytes 384 | tf_op jit(solution)/shard_map/psum | solution.py:168
  414.9 2.7 multiply_reduce_fusion.5
  417.6 56.2 %psum.69 = f32[16]{0:T(128)S(1)} all-reduce(f32[16]{0:T(128)S(1)} %get-tuple-element.19), channel_id=1, replica_groups=mesh['grp'=8,'cell'=32] {'cell'}, use_global_device_ids=true, to_apply=%region_16.17 | all-reduce | flops 16 | bytes 128 | tf_op jit(solution)/shard_map/psum | solution.py:171
  473.8 1.4 copy_divide_fusion
  475.6 1.4 collective-permute-start.8
  477.0 4.1 collective-permute-start.9
  481.2 0.6 multiply_multiply_fusion.8
  482.3 0.8 collective-permute-done.9
  483.4 0.5 fusion.28
  484.8 0.6 copy-done.8
  485.4 0.7 multiply_reduce_fusion.4
  486.2 57.4 %psum.70 = f32[4,16]{1,0:T(4,128)S(1)} all-reduce(f32[4,16]{1,0:T(4,128)S(1)} %pad_maximum_fusion.13), channel_id=1, replica_groups=mesh['grp'=8,'cell'=32] {'cell'}, use_global_device_ids=true, to_apply=%region_21.22 | all-reduce | flops 64 | bytes 512 | tf_op jit(solution)/shard_map/psum | solution.py:168
  543.6 2.2 multiply_reduce_fusion
  545.8 56.0 %psum.71 = f32[16]{0:T(128)S(1)} all-reduce(f32[16]{0:T(128)S(1)} %multiply_reduce_fusion), channel_id=1, replica_groups=mesh['grp'=8,'cell'=32] {'cell'}, use_global_device_ids=true, to_apply=%region_23.24 | all-reduce | flops 16 | bytes 128 | tf_op jit(solution)/shard_map/psum | solution.py:171
  601.9 1.8 multiply_add_fusion
  603.9 0.8 copy-done.43
  604.9 4.6 copy.165
  609.5 4.1 gather_fusion.1
  613.7 36.3 %all_gather.10 = f32[32,16,256]{2,1,0:T(8,128)S(1)} all-gather(f32[1,16,256]{2,1,0:T(8,128)S(1)} %fusion.85), channel_id=1, replica_groups=mesh['grp'=8,'cell'=32] {'cell'}, dimensions={0}, use_global_device_ids=true | all-gather | bytes 540672 | tf_op jit(solution)/shard_map/all_gather | solution.py:12
  650.1 156.6 %all_gather.11 = f32[128,256]{1,0:T(8,128)S(1)} all-gather(f32[16,256]{1,0:T(8,128)S(1)} %reduce_sum.168), channel_id=1, replica_groups=mesh['grp'=8,'cell'=32] {'grp'}, dimensions={0}, use_global_device_ids=true | all-gather | bytes 147456 | tf_op jit(solution)/shard_map/all_gather | solution.py:189
  807.1 11.7 %cholesky.17 = f32[128,128]{1,0:T(8,128)S(1)} custom-call(f32[128,128]{1,0:T(8,128)S(1)} %fusion.78), custom_call_target="Cholesky" | custom-call | tf_op jit(solution)/shard_map/jit(cholesky)/cholesky | solution.py:123
  818.9 0.6 compare_reduce_fusion
  819.5 0.7 fusion.72
  820.2 9.8 %custom-call.10 = f32[1,128,128]{1,2,0:T(8,128)S(1)} custom-call(f32[1,128,128]{2,1,0:T(8,128)S(1)} %fusion.72), custom_call_target="InvertDiagBlocksLowerTriangular" | custom-call | tf_op jit(solution)/shard_map/jit(_cho_solve)/triangular_solve | solution.py:124
  831.0 7.1 fusion
  838.3 1.1 slice_bitcast_fusion.1
  (189 shorter events, 12.3 us)
Async XLA Ops:
  7.2 82.7 %copy-start = (s32[128]{0:T(128)S(1)}, s32[128]{0:T(128)}, u32[]{:S(2)}) copy-start(s32[128]{0:T(128)} %param.18) | copy-start | bytes 1540
  7.2 6.6 copy-start.2
  7.2 823.7 %all-gather.2.cloned.1.call-start = ((), (), s32[]{:S(2)}) async-start(), calls=%async_computation | async-start | bytes 9437184 | tf_op jit(solution)/shard_map/all_gather | solution.py:198
  9.3 77.7 %copy-start.5 = (f32[16,4,16,128]{3,2,1,0:T(8,128)S(1)}, f32[16,4,16,128]{3,2,1,0:T(8,128)}, u32[]{:S(2)}) copy-start(f32[16,4,16,128]{3,2,1,0:T(8,128)} %param.12) | copy-start | bytes 1572868
  9.3 77.7 %copy-start.37 = (f32[16,4,16,128]{3,2,1,0:T(8,128)S(1)}, f32[16,4,16,128]{3,2,1,0:T(8,128)}, u32[]{:S(2)}) copy-start(f32[16,4,16,128]{3,2,1,0:T(8,128)} %param.11) | copy-start | bytes 1572868
  9.3 86.4 %collective-permute-start = (f32[16,2,1,16,128]{4,3,2,0,1:T(8,128)}, f32[16,2,1,16,128]{4,3,2,0,1:T(8,128)S(1)}, u32[]{:S(2)}, u32[]{:S(2)}) collective-permute-start(f32[16,2,1,16,128]{4,3,2,0,1:T(8,128)} %get-tuple-element.67), channel_id=1, source_target_pairs={{0,1},{1,2},{2,3},{3,4},{4,5},{5,6},{6,7},{7,8},{8,9},{9,10},{10,1... | collective-permute-start | bytes 786440 | tf_op jit(solution)/shard_map/ppermute | solution.py:20
  14.0 81.7 %collective-permute-start.1 = (f32[16,2,1,16,128]{4,3,2,0,1:T(8,128)}, f32[16,2,1,16,128]{4,3,2,0,1:T(8,128)}, u32[]{:S(2)}, u32[]{:S(2)}) collective-permute-start(f32[16,2,1,16,128]{4,3,2,0,1:T(8,128)} %get-tuple-element.68), channel_id=1, source_target_pairs={{1,0},{2,1},{3,2},{4,3},{5,4},{6,5},{7,6},{8,7},{9,8},{10,9},{11,1... | collective-permute-start | bytes 786440 | tf_op jit(solution)/shard_map/ppermute | solution.py:23
  81.0 20.7 %collective-permute-start.2 = (f32[16,1,16,128]{3,2,1,0:T(8,128)}, f32[16,1,16,128]{3,2,1,0:T(8,128)}, u32[]{:S(2)}, u32[]{:S(2)}) collective-permute-start(f32[16,1,16,128]{3,2,1,0:T(8,128)} %get-tuple-element.81), channel_id=1, source_target_pairs={{1,0},{2,1},{3,2},{4,3},{5,4},{6,5},{7,6},{8,7},{9,8},{10,9},{11,1... | collective-permute-start | bytes 393224 | tf_op jit(solution)/shard_map/ppermute | solution.py:23
  82.3 19.4 %collective-permute-start.3 = (f32[16,1,16,128]{3,2,1,0:T(8,128)}, f32[16,1,16,128]{3,2,1,0:T(8,128)}, u32[]{:S(2)}, u32[]{:S(2)}) collective-permute-start(f32[16,1,16,128]{3,2,1,0:T(8,128)} %get-tuple-element.82), channel_id=1, source_target_pairs={{0,1},{1,2},{2,3},{3,4},{4,5},{5,6},{6,7},{7,8},{8,9},{9,10},{10,1... | collective-permute-start | bytes 393224 | tf_op jit(solution)/shard_map/ppermute | solution.py:20
  87.1 1.0 copy-start.22
  88.1 1.8 copy-start.45
  89.9 3.8 copy-start.3
  92.7 2.9 copy-start.46
  96.9 1.0 copy-start.31
  96.9 1.2 copy-start.32
  97.0 1.3 copy-start.33
  97.0 1.5 copy-start.34
  99.6 1.6 copy-start.12
  99.6 128.1 %copy-start.9 = (f32[16,4,16,128]{3,2,1,0:T(8,128)}, f32[16,4,16,128]{3,2,1,0:T(8,128)S(1)}, u32[]{:S(2)}) copy-start(f32[16,4,16,128]{3,2,1,0:T(8,128)S(1)} %get-tuple-element.26) | copy-start | bytes 1572868
  104.9 0.8 copy-start.35
  105.7 0.8 copy-start.36
  221.9 5.8 copy-start.13
  221.9 5.8 copy-start.24
  221.9 5.8 copy-start.27
  222.3 6.5 collective-permute-start.4
  223.7 5.9 collective-permute-start.5
  228.3 1.3 copy-start.16
  228.3 1.3 copy-start.19
  230.4 0.8 copy-start.41
  231.2 0.8 copy-start.42
  347.2 6.0 copy-start.10
  347.2 6.0 copy-start.14
  347.2 6.0 copy-start.25
  347.2 6.0 copy-start.28
  347.6 6.8 collective-permute-start.6
  349.0 6.0 collective-permute-start.7
  353.8 1.1 copy-start.17
  353.8 1.3 copy-start.20
  354.3 1.1 copy-start.6
  356.0 0.8 copy-start.39
  356.8 0.8 copy-start.40
  475.2 5.9 copy-start.11
  475.3 5.9 copy-start.15
  475.3 5.9 copy-start.26
  475.3 5.9 copy-start.29
  475.6 6.7 collective-permute-start.8
  477.0 6.1 collective-permute-start.9
  481.8 1.3 copy-start.18
  481.8 1.3 copy-start.21
  482.3 1.1 copy-start.7
  484.0 0.8 copy-start.38
  484.0 1.4 copy-start.8
  485.4 0.8 copy-start.30
  601.9 1.8 copy-start.4
  601.9 1.8 copy-start.44
  603.8 1.0 copy-start.43
  609.5 220.5 %copy-start.47 = (f32[128,256]{1,0:T(8,128)S(1)}, f32[128,256]{1,0:T(8,128)}, u32[]{:S(2)}) copy-start(f32[128,256]{1,0:T(8,128)} %param.17) | copy-start | bytes 393220
  609.5 220.6 %copy-start.48 = (f32[256]{0:T(256)S(1)}, f32[256]{0:T(256)}, u32[]{:S(2)}) copy-start(f32[256]{0:T(256)} %param.15) | copy-start | bytes 3076
  650.0 180.9 %copy-start.23 = (f32[16,2,4,16,128]{4,3,2,1,0:T(8,128)S(1)}, f32[16,2,4,16,128]{4,3,2,1,0:T(8,128)}, u32[]{:S(2)}) copy-start(f32[16,2,4,16,128]{4,3,2,1,0:T(8,128)} %copy-done.22) | copy-start | bytes 3145732
  838.0 1.3 copy-start.1
Sparse Core Ops, SparseCore 0:
  89.9 61.6 all-gather.1
